TPU v7x, 256 devices: a whole 4x4x8 slice. The times are simulated.
256 devices in a mesh: shell: 4 (over x_lo, core), tile: 64 (over z, x_hi, y).
Axes of the slice: x: 4 (x_hi: 2, x_lo: 2; x = x_hi * 2 + x_lo), y: 4, z: 8, core: 2. Of those that a mesh axis runs over, the one named last changes fastest.
Arguments:
- latent: float32 [64, 2048, 512], P('shell', 'tile'), may hold values from -5 to 5
- shell_sigma: float32 [64], P('shell'), may hold values from 0.15 to 0.6
- lens_weight: float32 [5, 64], P(None, 'shell'), may hold values from 0 to 0.5
- shear_kernel: bfloat16 [2, 33, 33], replicated, may hold values from -0.1875 to 0.1875
- star_mask: int32 [2048, 512], P('tile', 'shell'), may hold values 0 or 1
- gal_pix: int32 [16, 4096, 128], P('shell', 'tile'), may hold values from 0 to 4095
- gal_bin: int32 [16, 4096, 128], P('shell', 'tile'), may hold values from 0 to 4
- gal_shape: float32 [2, 16, 4096, 128], P(None, 'shell', 'tile'), may hold values from -3 to 3
- gal_weight: float32 [16, 4096, 128], P('shell', 'tile'), may hold values from 0.5 to 4
- gal_counts: int32 [16, 4096], P('shell', 'tile'), may hold values from 0 to 128, as said below
Outputs:
- grad_field: float32 [64, 2048, 512], P('shell', 'tile')
Inputs may be any that keep to these rules, and one draw needn't show every extreme that they name: Bucket (i, j) of the galaxy arrays holds galaxies for the tile j mod 64 and the column block i mod 4, in its first gal_counts[i, j] slots; in every draw some destination block receives 128 galaxies from every device, and buckets' loads range from near zero to 128.
All inputs are finite; a program needn't handle non-finite values. No bound on the sum of `star_mask` on one device may be relied on, other than what follows from the above.
Results may differ from a plain program's by a relative error of at most 0.0023.
Values may be sent and summed in bfloat16 or wider, within the bound.
No kernel may reach another device: no remote copies, remote signals or barrier semaphores. Data moves between devices by JAX's collectives and lax.ppermute only.
A program may use at most 64 MiB of HBM per device.

v0:
```python
import jax
import jax.numpy as jnp
from jax import lax
from jax.sharding import PartitionSpec as P

NBIN = 5
KER = 33
HALF = 16


def extended(block, sides, width):
    for axis, dim in sides:
        count = lax.axis_size(axis)
        forward = [(i, i + 1) for i in range(count - 1)]
        backward = [(target, source) for source, target in forward]
        low = lax.ppermute(
            lax.slice_in_dim(block, block.shape[dim] - width, None, axis=dim), axis, forward
        )
        high = lax.ppermute(lax.slice_in_dim(block, 0, width, axis=dim), axis, backward)
        block = jnp.concatenate([low, block, high], axis=dim)
    return block


def build_bands(kernel, columns):
    span = columns + KER - 1
    grid_shape = (KER, span, columns)
    lagged = lax.broadcasted_iota(jnp.int32, grid_shape, 1) - lax.broadcasted_iota(
        jnp.int32, grid_shape, 2
    )
    onehot = (lagged == lax.broadcasted_iota(jnp.int32, grid_shape, 0)).astype(jnp.bfloat16)
    bands = jnp.einsum("kdv,vjc->kdjc", kernel, onehot, preferred_element_type=jnp.float32)
    return bands.astype(jnp.bfloat16)


def stacked_rows(padded, height):
    return jnp.stack([padded[..., offset : offset + height, :] for offset in range(KER)], axis=-3)


def deposit_block(shear_rows, codes, observed, weights, columns):
    row_count = shear_rows.shape[1]
    usable = codes >= 0
    safe_codes = jnp.where(usable, codes, 0)
    row_of = safe_codes // columns
    col_of = safe_codes % columns
    rows_hot = (
        row_of[:, None] == lax.broadcasted_iota(jnp.int32, (codes.shape[0], row_count), 1)
    ).astype(jnp.float32)
    cols_hot = (
        col_of[:, None] == lax.broadcasted_iota(jnp.int32, (codes.shape[0], columns), 1)
    ).astype(jnp.float32)
    picked = jnp.einsum(
        "gr,krc->kgc",
        rows_hot,
        shear_rows,
        precision=lax.Precision.HIGHEST,
        preferred_element_type=jnp.float32,
    )
    predicted = jnp.sum(picked * cols_hot[None], axis=2)
    scaled = jnp.where(usable, weights, 0.0)
    residual = scaled[None] * (predicted - observed)
    spread = residual[:, :, None] * cols_hot[None]
    return jnp.einsum(
        "gr,kgc->krc",
        rows_hot,
        spread,
        precision=lax.Precision.HIGHEST,
        preferred_element_type=jnp.float32,
    )


def per_device(
    latent,
    shell_sigma,
    lens_weight,
    shear_kernel,
    star_mask,
    gal_pix,
    gal_bin,
    gal_shape,
    gal_weight,
    gal_counts,
):
    height = latent.shape[1]
    width = latent.shape[2]
    shell_count = lax.axis_size("shell")
    columns = width // shell_count
    pixels = height * columns
    sigma = shell_sigma[:, None, None]
    growth = jnp.exp(sigma * latent - 0.5 * sigma * sigma)
    partial_bins = jnp.einsum(
        "bs,srw->brw",
        lens_weight,
        growth - 1.0,
        precision=lax.Precision.HIGHEST,
        preferred_element_type=jnp.float32,
    )
    bin_map = lax.psum_scatter(partial_bins, "shell", scatter_dimension=2, tiled=True).astype(
        jnp.bfloat16
    )
    padded = extended(bin_map, (("shell", 2), ("tile", 1)), HALF)
    forward_bands = build_bands(shear_kernel, columns)
    shear = jnp.einsum(
        "bdrj,kdjc->kbrc",
        stacked_rows(padded, height),
        forward_bands,
        preferred_element_type=jnp.float32,
    )
    slot_index = lax.broadcasted_iota(jnp.int32, gal_pix.shape, 2)
    codes = jnp.where(slot_index < gal_counts[:, :, None], gal_bin * pixels + gal_pix, -1).astype(
        jnp.float32
    )
    packet = jnp.concatenate([codes[None], gal_shape, gal_weight[None]], axis=0)
    arrived = lax.all_to_all(
        lax.all_to_all(packet, "shell", split_axis=1, concat_axis=1, tiled=True),
        "tile",
        split_axis=2,
        concat_axis=2,
        tiled=True,
    )
    shear_rows = shear.reshape(2, NBIN * height, columns)
    groups = arrived.shape[1]

    def add_group(group, total):
        block = lax.dynamic_index_in_dim(arrived, group, 1, keepdims=False).reshape(4, -1)
        group_codes = block[0].astype(jnp.int32)
        return total + deposit_block(shear_rows, group_codes, block[1:3], block[3], columns)

    summed = lax.fori_loop(0, groups, add_group, jnp.zeros_like(shear_rows))
    shear_grad = summed.reshape(2, NBIN, height, columns)
    masked = (shear_grad * star_mask.astype(jnp.float32)).astype(jnp.bfloat16)
    rims = extended(masked, (("shell", 3), ("tile", 2)), HALF)
    back_bands = build_bands(jnp.flip(shear_kernel, (1, 2)), columns)
    bin_grad = jnp.einsum(
        "kbdrj,kdjc->brc",
        stacked_rows(rims, height),
        back_bands,
        preferred_element_type=jnp.float32,
    )
    full_grad = lax.all_gather(bin_grad, "shell", axis=2, tiled=True)
    mixed = jnp.einsum(
        "bs,brw->srw",
        lens_weight,
        full_grad,
        precision=lax.Precision.HIGHEST,
        preferred_element_type=jnp.float32,
    )
    return sigma * growth * mixed


def solution(mesh):
    return jax.shard_map(
        per_device,
        mesh=mesh,
        in_specs=(
            P("shell", "tile", None),
            P("shell"),
            P(None, "shell"),
            P(),
            P("tile", "shell"),
            P("shell", "tile", None),
            P("shell", "tile", None),
            P(None, "shell", "tile", None),
            P("shell", "tile", None),
            P("shell", "tile"),
        ),
        out_specs=P("shell", "tile", None),
        check_vma=False,
    )
```

profile of v0, /device:TPU:31, one launch (start us, length us, event | category | flops | bytes accessed | tf_op | source)
XLA Modules:
  0.0 210.8 jit_solution(7721434345518271787)
XLA Ops:
  7.2 3.4 %convolution_bitcast_fusion.1 = f32[5,32,512]{2,0,1:T(8,128)} fusion(f32[16,32,512]{2,1,0:T(8,128)} %param.12, f32[16]{0:T(128)S(1)} %multiply_multiply_fusion, f32[16]{0:T(128)} %param.13, f32[5,16]{1,0:T(8,128)S(1)} %copy-done), kind=kOutput, calls=%fused_computation.44 | convolution fusion | flops 16515072 | bytes 1376704 | tf_op jit(solution)/shard_map/bs,srw->brw/dot_general | solution.py:90
  12.8 21.4 %reduce-scatter.2.cloned.1.call-done = f32[5,32,128]{2,0,1:T(8,128)} async-done(((f32[5,32,512]{2,0,1:T(8,128)}), f32[5,32,128]{2,0,1:T(8,128)}) %reduce-scatter.2.cloned.1.call-update) | async-done | bytes 81936 | tf_op jit(solution)/shard_map/reduce_scatter | solution.py:97
  36.5 3.0 %collective-permute-start.1 = (bf16[5,32,16]{2,0,1:T(8,128)(2,1)S(1)}, bf16[5,32,16]{2,0,1:T(8,128)(2,1)S(1)}, u32[]{:S(2)}, u32[]{:S(2)}) collective-permute-start(bf16[5,32,16]{2,0,1:T(8,128)(2,1)S(1)} %get-tuple-element.165), channel_id=1, source_target_pairs={{64,0},{128,64},{192,128},{65,1},{129,65},{193,129},{66,2},{130,66... | collective-permute-start | bytes 15368 | tf_op jit(solution)/shard_map/ppermute | solution.py:19
  39.6 2.1 pad_maximum_fusion
  41.7 4.2 %all-to-all-start = ((f32[4,4,64,128]{3,0,2,1:T(4,128)}), f32[4,4,64,128]{3,0,2,1:T(4,128)}, u32[]{:S(2)}, u32[]{:S(2)}) async-start(f32[4,4,64,128]{3,0,2,1:T(4,128)} %pad_maximum_fusion), calls=%async_computation | async-start | bytes 1048576 | tf_op jit(solution)/shard_map/all_to_all | solution.py:114
  46.7 4.0 %collective-permute-start.2 = (bf16[5,16,160]{2,0,1:T(8,128)(2,1)}, bf16[5,16,160]{2,0,1:T(8,128)(2,1)}, u32[]{:S(2)}, u32[]{:S(2)}) collective-permute-start(bf16[5,16,160]{2,0,1:T(8,128)(2,1)} %get-tuple-element.161), channel_id=1, source_target_pairs={{0,1},{1,2},{2,3},{3,4},{4,5},{5,6},{6,7},{7,8},{8,9},{9,10},{10,1... | collective-permute-start | bytes 76808 | tf_op jit(solution)/shard_map/ppermute | solution.py:16
  50.7 1.9 collective-permute-start.3
  53.7 1.9 copy.27
  55.6 13.7 %all-to-all-start.1 = ((f32[4,4,64,128]{3,0,1,2:T(4,128)}), f32[4,4,64,128]{3,0,1,2:T(4,128)}, u32[]{:S(2)}, u32[]{:S(2)}) async-start(f32[4,4,64,128]{3,0,1,2:T(4,128)} %copy.27), calls=%async_computation.1 | async-start | bytes 1048576 | tf_op jit(solution)/shard_map/all_to_all | solution.py:113
  71.1 1.6 fusion.34
  72.8 11.5 %all-to-all-done.1 = f32[4,4,64,128]{3,0,1,2:T(4,128)} async-done(((f32[4,4,64,128]{3,0,1,2:T(4,128)}), f32[4,4,64,128]{3,0,1,2:T(4,128)}, u32[]{:S(2)}, u32[]{:S(2)}) %all-to-all-start.1) | async-done | bytes 524320 | tf_op jit(solution)/shard_map/all_to_all | solution.py:113
  84.3 79.2 %while.16 = (s32[]{:T(128)}, f32[2,160,128]{2,1,0:T(8,128)}, f32[4,4,64,128]{3,0,1,2:T(4,128)}, f32[2,160,128]{2,1,0:T(8,128)S(1)}, s32[]{:T(128)}, /*index=5*/s32[]{:T(128)}, s32[]{}, s32[]{}) while((s32[]{:T(128)}, f32[2,160,128]{2,1,0:T(8,128)}, f32[4,4,64,128]{3,0,1,2:T(4,128)}, f32[2,160,128]{2,1,0:T(8,128)S(1)}, s32[]{:T(128)}, ...), condition=%wide.region_3.4_spmd.clone, body=%wide.region_1.3_spmd.clone.sunk | while | flops 8064376832 | bytes 40337624 | solution.py:128
  85.8 4.4 %fusion.112 = f32[8192,2]{0,1:T(2,128)S(1)} fusion(f32[8192,128]{0,1:T(8,128)S(1)} %fusion.111, f32[2,160,128]{2,1,0:T(8,128)S(1)} %get-tuple-element.218, s32[8192]{0:T(1024)S(1)} %get-tuple-element.196), kind=kOutput, calls=%fused_computation.11.clone.1 | convolution fusion | flops 4032020480 | bytes 4456448 | tf_op jit(solution)/shard_map/while/body/eval_jaxpr/gr,krc->kgc/dot_general | solution.py:51
  91.3 5.6 %copy.80 = f32[8192,128]{1,0:T(8,128)} copy(f32[8192,128]{0,1:T(8,128)} %copy-done.1) | data formatting | bytes 8388608 | tf_op jit(solution)/shard_map/while/body/eval_jaxpr/convert_element_type | solution.py:50
  96.9 6.6 %fusion.114 = f32[2,160,128]{2,1,0:T(8,128)S(1)} fusion(s32[8192]{0:T(1024)S(1)} %get-tuple-element.196, f32[8192,128]{1,0:T(8,128)} %copy.80, f32[2,8192]{1,0:T(2,128)S(1)} %fusion.113, f32[2,160,128]{2,1,0:T(8,128)S(1)} %copy-done.3, pred[]{:T(512)S(6)} %compare.19), kind=kOutput, calls=%fused_computation.13.clone.1 | convolution fusion | flops 4030021632 | bytes 4620289 | tf_op jit(solution)/shard_map/while/body/eval_jaxpr/gr,kgc->krc/dot_general | solution.py:62
  105.6 4.4 %fusion.112 = f32[8192,2]{0,1:T(2,128)S(1)} fusion(f32[8192,128]{0,1:T(8,128)S(1)} %fusion.111, f32[2,160,128]{2,1,0:T(8,128)S(1)} %get-tuple-element.218, s32[8192]{0:T(1024)S(1)} %get-tuple-element.196), kind=kOutput, calls=%fused_computation.11.clone.1 | convolution fusion | flops 4032020480 | bytes 4456448 | tf_op jit(solution)/shard_map/while/body/eval_jaxpr/gr,krc->kgc/dot_general | solution.py:51
  111.1 5.6 %copy.80 = f32[8192,128]{1,0:T(8,128)} copy(f32[8192,128]{0,1:T(8,128)} %copy-done.1) | data formatting | bytes 8388608 | tf_op jit(solution)/shard_map/while/body/eval_jaxpr/convert_element_type | solution.py:50
  116.7 6.6 %fusion.114 = f32[2,160,128]{2,1,0:T(8,128)S(1)} fusion(s32[8192]{0:T(1024)S(1)} %get-tuple-element.196, f32[8192,128]{1,0:T(8,128)} %copy.80, f32[2,8192]{1,0:T(2,128)S(1)} %fusion.113, f32[2,160,128]{2,1,0:T(8,128)S(1)} %copy-done.3, pred[]{:T(512)S(6)} %compare.19), kind=kOutput, calls=%fused_computation.13.clone.1 | convolution fusion | flops 4030021632 | bytes 4620289 | tf_op jit(solution)/shard_map/while/body/eval_jaxpr/gr,kgc->krc/dot_general | solution.py:62
  125.4 4.4 %fusion.112 = f32[8192,2]{0,1:T(2,128)S(1)} fusion(f32[8192,128]{0,1:T(8,128)S(1)} %fusion.111, f32[2,160,128]{2,1,0:T(8,128)S(1)} %get-tuple-element.218, s32[8192]{0:T(1024)S(1)} %get-tuple-element.196), kind=kOutput, calls=%fused_computation.11.clone.1 | convolution fusion | flops 4032020480 | bytes 4456448 | tf_op jit(solution)/shard_map/while/body/eval_jaxpr/gr,krc->kgc/dot_general | solution.py:51
  130.9 5.6 %copy.80 = f32[8192,128]{1,0:T(8,128)} copy(f32[8192,128]{0,1:T(8,128)} %copy-done.1) | data formatting | bytes 8388608 | tf_op jit(solution)/shard_map/while/body/eval_jaxpr/convert_element_type | solution.py:50
  136.5 6.6 %fusion.114 = f32[2,160,128]{2,1,0:T(8,128)S(1)} fusion(s32[8192]{0:T(1024)S(1)} %get-tuple-element.196, f32[8192,128]{1,0:T(8,128)} %copy.80, f32[2,8192]{1,0:T(2,128)S(1)} %fusion.113, f32[2,160,128]{2,1,0:T(8,128)S(1)} %copy-done.3, pred[]{:T(512)S(6)} %compare.19), kind=kOutput, calls=%fused_computation.13.clone.1 | convolution fusion | flops 4030021632 | bytes 4620289 | tf_op jit(solution)/shard_map/while/body/eval_jaxpr/gr,kgc->krc/dot_general | solution.py:62
  145.2 4.4 %fusion.112 = f32[8192,2]{0,1:T(2,128)S(1)} fusion(f32[8192,128]{0,1:T(8,128)S(1)} %fusion.111, f32[2,160,128]{2,1,0:T(8,128)S(1)} %get-tuple-element.218, s32[8192]{0:T(1024)S(1)} %get-tuple-element.196), kind=kOutput, calls=%fused_computation.11.clone.1 | convolution fusion | flops 4032020480 | bytes 4456448 | tf_op jit(solution)/shard_map/while/body/eval_jaxpr/gr,krc->kgc/dot_general | solution.py:51
  150.7 5.6 %copy.80 = f32[8192,128]{1,0:T(8,128)} copy(f32[8192,128]{0,1:T(8,128)} %copy-done.1) | data formatting | bytes 8388608 | tf_op jit(solution)/shard_map/while/body/eval_jaxpr/convert_element_type | solution.py:50
  156.3 6.6 %fusion.114 = f32[2,160,128]{2,1,0:T(8,128)S(1)} fusion(s32[8192]{0:T(1024)S(1)} %get-tuple-element.196, f32[8192,128]{1,0:T(8,128)} %copy.80, f32[2,8192]{1,0:T(2,128)S(1)} %fusion.113, f32[2,160,128]{2,1,0:T(8,128)S(1)} %copy-done.3, pred[]{:T(512)S(6)} %compare.19), kind=kOutput, calls=%fused_computation.13.clone.1 | convolution fusion | flops 4030021632 | bytes 4620289 | tf_op jit(solution)/shard_map/while/body/eval_jaxpr/gr,kgc->krc/dot_general | solution.py:62
  165.8 5.4 %collective-permute-start.5 = (bf16[2,5,32,16]{3,2,1,0:T(8,128)(2,1)S(1)}, bf16[2,5,32,16]{3,2,1,0:T(8,128)(2,1)S(1)}, u32[]{:S(2)}, u32[]{:S(2)}) collective-permute-start(bf16[2,5,32,16]{3,2,1,0:T(8,128)(2,1)S(1)} %get-tuple-element.163), channel_id=1, source_target_pairs={{64,0},{128,64},{192,128},{65,1},{129,65},{193,129},{66,2},{130,66... | collective-permute-start | bytes 30728 | tf_op jit(solution)/shard_map/ppermute | solution.py:19
  172.3 5.0 %collective-permute-start.6 = (bf16[2,5,16,160]{3,2,1,0:T(8,128)(2,1)S(1)}, bf16[2,5,16,160]{3,2,1,0:T(8,128)(2,1)S(1)}, u32[]{:S(2)}, u32[]{:S(2)}) collective-permute-start(bf16[2,5,16,160]{3,2,1,0:T(8,128)(2,1)S(1)} %get-tuple-element.159), channel_id=1, source_target_pairs={{0,1},{1,2},{2,3},{3,4},{4,5},{5,6},{6,7},{7,8},{8,9},{9,10},{10,1... | collective-permute-start | bytes 153608 | tf_op jit(solution)/shard_map/ppermute | solution.py:16
  177.3 2.1 %collective-permute-start.7 = (bf16[2,5,16,160]{3,2,1,0:T(8,128)(2,1)S(1)}, bf16[2,5,16,160]{3,2,1,0:T(8,128)(2,1)S(1)}, u32[]{:S(2)}, u32[]{:S(2)}) collective-permute-start(bf16[2,5,16,160]{3,2,1,0:T(8,128)(2,1)S(1)} %get-tuple-element.158), channel_id=1, source_target_pairs={{1,0},{2,1},{3,2},{4,3},{5,4},{6,5},{7,6},{8,7},{9,8},{10,9},{11,1... | collective-permute-start | bytes 153608 | tf_op jit(solution)/shard_map/ppermute | solution.py:19
  180.5 6.5 %collective-permute-done.7 = bf16[2,5,16,160]{3,2,1,0:T(8,128)(2,1)S(1)} collective-permute-done((bf16[2,5,16,160]{3,2,1,0:T(8,128)(2,1)S(1)}, bf16[2,5,16,160]{3,2,1,0:T(8,128)(2,1)S(1)}, u32[]{:S(2)}, u32[]{:S(2)}) %collective-permute-start.7) | collective-permute-done | bytes 51232 | tf_op jit(solution)/shard_map/ppermute | solution.py:19
  189.0 1.6 fusion.43
  190.6 10.1 %all_gather.3 = f32[5,32,512]{2,1,0:T(8,128)S(1)} all-gather(f32[5,32,128]{2,1,0:T(8,128)S(1)} %fusion.43), channel_id=1, replica_groups=mesh['shell'=4,'tile'=64] {'shell'}, dimensions={2}, use_global_device_ids=true | all-gather | bytes 409600 | tf_op jit(solution)/shard_map/all_gather | solution.py:139
  200.7 1.7 fusion.42
  202.3 1.6 copy.35
  (150 shorter events, 27.4 us)
Async XLA Ops:
  6.5 0.7 copy-start
  6.5 46.1 %copy-start.5 = (bf16[2,33,33]{2,0,1:T(2,128)(2,1)S(1)}, bf16[2,33,33]{2,0,1:T(2,128)(2,1)}, u32[]{:S(2)}) copy-start(bf16[2,33,33]{2,0,1:T(2,128)(2,1)} %param.15) | copy-start | bytes 13072
  6.5 27.7 %reduce-scatter.2.cloned.1.call-start = ((), (), s32[]{:S(2)}) async-start(), calls=%async_computation.3 | async-start | bytes 655360 | tf_op jit(solution)/shard_map/reduce_scatter | solution.py:97
  10.6 43.1 %copy-start.6 = (s32[32,128]{1,0:T(8,128)S(1)}, s32[32,128]{1,0:T(8,128)}, u32[]{:S(2)}) copy-start(s32[32,128]{1,0:T(8,128)} %param.16) | copy-start | bytes 49156
  35.2 10.7 %collective-permute-start = (bf16[5,32,16]{2,0,1:T(8,128)(2,1)S(1)}, bf16[5,32,16]{2,0,1:T(8,128)(2,1)S(1)}, u32[]{:S(2)}, u32[]{:S(2)}) collective-permute-start(bf16[5,32,16]{2,0,1:T(8,128)(2,1)S(1)} %get-tuple-element.164), channel_id=1, source_target_pairs={{0,64},{64,128},{128,192},{1,65},{65,129},{129,193},{2,66},{66,130... | collective-permute-start | bytes 15368 | tf_op jit(solution)/shard_map/ppermute | solution.py:16
  36.5 9.4 %collective-permute-start.1 = (bf16[5,32,16]{2,0,1:T(8,128)(2,1)S(1)}, bf16[5,32,16]{2,0,1:T(8,128)(2,1)S(1)}, u32[]{:S(2)}, u32[]{:S(2)}) collective-permute-start(bf16[5,32,16]{2,0,1:T(8,128)(2,1)S(1)} %get-tuple-element.165), channel_id=1, source_target_pairs={{64,0},{128,64},{192,128},{65,1},{129,65},{193,129},{66,2},{130,66... | collective-permute-start | bytes 15368 | tf_op jit(solution)/shard_map/ppermute | solution.py:19
  41.7 12.1 %all-to-all-start = ((f32[4,4,64,128]{3,0,2,1:T(4,128)}), f32[4,4,64,128]{3,0,2,1:T(4,128)}, u32[]{:S(2)}, u32[]{:S(2)}) async-start(f32[4,4,64,128]{3,0,2,1:T(4,128)} %pad_maximum_fusion), calls=%async_computation | async-start | bytes 1048576 | tf_op jit(solution)/shard_map/all_to_all | solution.py:114
  46.7 22.6 %collective-permute-start.2 = (bf16[5,16,160]{2,0,1:T(8,128)(2,1)}, bf16[5,16,160]{2,0,1:T(8,128)(2,1)}, u32[]{:S(2)}, u32[]{:S(2)}) collective-permute-start(bf16[5,16,160]{2,0,1:T(8,128)(2,1)} %get-tuple-element.161), channel_id=1, source_target_pairs={{0,1},{1,2},{2,3},{3,4},{4,5},{5,6},{6,7},{7,8},{8,9},{9,10},{10,1... | collective-permute-start | bytes 76808 | tf_op jit(solution)/shard_map/ppermute | solution.py:16
  50.7 18.6 %collective-permute-start.3 = (bf16[5,16,160]{2,0,1:T(8,128)(2,1)}, bf16[5,16,160]{2,0,1:T(8,128)(2,1)}, u32[]{:S(2)}, u32[]{:S(2)}) collective-permute-start(bf16[5,16,160]{2,0,1:T(8,128)(2,1)} %get-tuple-element.160), channel_id=1, source_target_pairs={{1,0},{2,1},{3,2},{4,3},{5,4},{6,5},{7,6},{8,7},{9,8},{10,9},{11,1... | collective-permute-start | bytes 76808 | tf_op jit(solution)/shard_map/ppermute | solution.py:19
  55.6 28.6 %all-to-all-start.1 = ((f32[4,4,64,128]{3,0,1,2:T(4,128)}), f32[4,4,64,128]{3,0,1,2:T(4,128)}, u32[]{:S(2)}, u32[]{:S(2)}) async-start(f32[4,4,64,128]{3,0,1,2:T(4,128)} %copy.27), calls=%async_computation.1 | async-start | bytes 1048576 | tf_op jit(solution)/shard_map/all_to_all | solution.py:113
  85.8 4.4 %copy-start.1 = (f32[8192,128]{0,1:T(8,128)}, f32[8192,128]{0,1:T(8,128)S(1)}, u32[]{:S(2)}) copy-start(f32[8192,128]{0,1:T(8,128)S(1)} %fusion.111) | copy-start | bytes 12582916 | tf_op jit(solution)/shard_map/while
  90.3 6.6 %copy-start.3 = (f32[2,160,128]{2,1,0:T(8,128)S(1)}, f32[2,160,128]{2,1,0:T(8,128)}, u32[]{:S(2)}) copy-start(f32[2,160,128]{2,1,0:T(8,128)} %get-tuple-element.208) | copy-start | bytes 491524 | tf_op jit(solution)/shard_map/while
  103.4 0.7 copy-start.4
  105.6 4.4 %copy-start.1 = (f32[8192,128]{0,1:T(8,128)}, f32[8192,128]{0,1:T(8,128)S(1)}, u32[]{:S(2)}) copy-start(f32[8192,128]{0,1:T(8,128)S(1)} %fusion.111) | copy-start | bytes 12582916 | tf_op jit(solution)/shard_map/while
  110.1 6.6 %copy-start.3 = (f32[2,160,128]{2,1,0:T(8,128)S(1)}, f32[2,160,128]{2,1,0:T(8,128)}, u32[]{:S(2)}) copy-start(f32[2,160,128]{2,1,0:T(8,128)} %get-tuple-element.208) | copy-start | bytes 491524 | tf_op jit(solution)/shard_map/while
  123.2 0.7 copy-start.4
  125.4 4.4 %copy-start.1 = (f32[8192,128]{0,1:T(8,128)}, f32[8192,128]{0,1:T(8,128)S(1)}, u32[]{:S(2)}) copy-start(f32[8192,128]{0,1:T(8,128)S(1)} %fusion.111) | copy-start | bytes 12582916 | tf_op jit(solution)/shard_map/while
  129.9 6.6 %copy-start.3 = (f32[2,160,128]{2,1,0:T(8,128)S(1)}, f32[2,160,128]{2,1,0:T(8,128)}, u32[]{:S(2)}) copy-start(f32[2,160,128]{2,1,0:T(8,128)} %get-tuple-element.208) | copy-start | bytes 491524 | tf_op jit(solution)/shard_map/while
  143.0 0.7 copy-start.4
  145.2 4.4 %copy-start.1 = (f32[8192,128]{0,1:T(8,128)}, f32[8192,128]{0,1:T(8,128)S(1)}, u32[]{:S(2)}) copy-start(f32[8192,128]{0,1:T(8,128)S(1)} %fusion.111) | copy-start | bytes 12582916 | tf_op jit(solution)/shard_map/while
  149.7 6.6 %copy-start.3 = (f32[2,160,128]{2,1,0:T(8,128)S(1)}, f32[2,160,128]{2,1,0:T(8,128)}, u32[]{:S(2)}) copy-start(f32[2,160,128]{2,1,0:T(8,128)} %get-tuple-element.208) | copy-start | bytes 491524 | tf_op jit(solution)/shard_map/while
  162.8 0.7 copy-start.4
  164.5 6.9 %collective-permute-start.4 = (bf16[2,5,32,16]{3,2,1,0:T(8,128)(2,1)S(1)}, bf16[2,5,32,16]{3,2,1,0:T(8,128)(2,1)S(1)}, u32[]{:S(2)}, u32[]{:S(2)}) collective-permute-start(bf16[2,5,32,16]{3,2,1,0:T(8,128)(2,1)S(1)} %get-tuple-element.162), channel_id=1, source_target_pairs={{0,64},{64,128},{128,192},{1,65},{65,129},{129,193},{2,66},{66,130... | collective-permute-start | bytes 30728 | tf_op jit(solution)/shard_map/ppermute | solution.py:16
  165.8 6.3 %collective-permute-start.5 = (bf16[2,5,32,16]{3,2,1,0:T(8,128)(2,1)S(1)}, bf16[2,5,32,16]{3,2,1,0:T(8,128)(2,1)S(1)}, u32[]{:S(2)}, u32[]{:S(2)}) collective-permute-start(bf16[2,5,32,16]{3,2,1,0:T(8,128)(2,1)S(1)} %get-tuple-element.163), channel_id=1, source_target_pairs={{64,0},{128,64},{192,128},{65,1},{129,65},{193,129},{66,2},{130,66... | collective-permute-start | bytes 30728 | tf_op jit(solution)/shard_map/ppermute | solution.py:19
  172.3 8.2 %collective-permute-start.6 = (bf16[2,5,16,160]{3,2,1,0:T(8,128)(2,1)S(1)}, bf16[2,5,16,160]{3,2,1,0:T(8,128)(2,1)S(1)}, u32[]{:S(2)}, u32[]{:S(2)}) collective-permute-start(bf16[2,5,16,160]{3,2,1,0:T(8,128)(2,1)S(1)} %get-tuple-element.159), channel_id=1, source_target_pairs={{0,1},{1,2},{2,3},{3,4},{4,5},{5,6},{6,7},{7,8},{8,9},{9,10},{10,1... | collective-permute-start | bytes 153608 | tf_op jit(solution)/shard_map/ppermute | solution.py:16
  177.3 9.7 %collective-permute-start.7 = (bf16[2,5,16,160]{3,2,1,0:T(8,128)(2,1)S(1)}, bf16[2,5,16,160]{3,2,1,0:T(8,128)(2,1)S(1)}, u32[]{:S(2)}, u32[]{:S(2)}) collective-permute-start(bf16[2,5,16,160]{3,2,1,0:T(8,128)(2,1)S(1)} %get-tuple-element.158), channel_id=1, source_target_pairs={{1,0},{2,1},{3,2},{4,3},{5,4},{6,5},{7,6},{8,7},{9,8},{10,9},{11,1... | collective-permute-start | bytes 153608 | tf_op jit(solution)/shard_map/ppermute | solution.py:19
  189.0 11.7 %copy-start.2 = (f32[16,32,512]{2,1,0:T(8,128)S(1)}, f32[16,32,512]{2,1,0:T(8,128)}, u32[]{:S(2)}) copy-start(f32[16,32,512]{2,1,0:T(8,128)} %param.12) | copy-start | bytes 3145732
  189.0 11.7 %copy-start.7 = (f32[16]{0:T(128)S(1)}, f32[16]{0:T(128)}, u32[]{:S(2)}) copy-start(f32[16]{0:T(128)} %param.13) | copy-start | bytes 196
Sparse Core Ops, SparseCore 0:
  10.7 23.4 reduce-scatter.1
where the time goes:
time: 212 us; the launch traced here: 211 us
  matrix products  54 us (25%)
  starting transfers between devices  42 us (20%)
  waiting for transfers between devices  40.2 us (19%)
  local copies, waits for them, and re-layouts  36.5 us (17%)
  between operations  14.2 us (7%)
  other arithmetic  13.4 us (6%)
  blocking collectives  10.1 us (5%)
    dot_general x4, matrix products, deposit_block(): jnp.einsum('gr,kgc->krc', rows_hot, spread, precision=lax.Precision.HIGHE...  26.2 us
    convert_element_type x4, local copies, waits for them, and re-layouts, deposit_block(): cols_hot = (col_of[:, None] == lax.broadcasted_iota(jnp.int32, (codes.sha...  22.3 us
    reduce_scatter x1, waiting for transfers between devices, per_device(): lax.psum_scatter(partial_bins, 'shell', scatter_dimension=2, tiled=True)  21.4 us
    dot_general x4, matrix products, deposit_block(): jnp.einsum('gr,krc->kgc', rows_hot, shear_rows, precision=lax.Precision.H...  17.6 us
    all_to_all x1, starting transfers between devices, per_device(): lax.all_to_all(lax.all_to_all(packet, 'shell', split_axis=1, concat_axis=...  13.7 us
    ppermute x4, starting transfers between devices, extended(): lax.ppermute(lax.slice_in_dim(block, 0, width, axis=dim), axis, backward)  12.5 us
    ppermute x4, starting transfers between devices, extended(): lax.ppermute(lax.slice_in_dim(block, block.shape[dim] - width, None, axis...  11.6 us
    all_to_all x1, waiting for transfers between devices, per_device(): lax.all_to_all(lax.all_to_all(packet, 'shell', split_axis=1, concat_axis=...  11.5 us
  transfers between devices with their start and end apart: 11, of which 4 were waited for; matrix products, arithmetic and copies ran while one was open for 6% of the time, Pallas kernels for 0%

commit v1 on v0

--- a/solution.py
+++ b/solution.py
@@ -1,11 +1,24 @@
+import functools
 import jax
 import jax.numpy as jnp
 from jax import lax
 from jax.sharding import PartitionSpec as P
+from jax.lax import all_to_all, axis_size
 
 NBIN = 5
 KER = 33
 HALF = 16
+
+
+def seats_all_recover(view, k_dim):
+    row_list = []
+    for _ in range(axis_size("shell")):
+        row_list.append(view)
+    field_out = all_to_all(jnp.stack(row_list), "shell", split_axis=0, concat_axis=0)
+    return jnp.concatenate(field_out, axis=k_dim)
+
+
+produce_orders = functools.partial(seats_all_recover, k_dim=2)
 
 
 def extended(block, sides, width):
@@ -136,7 +149,7 @@
         back_bands,
         preferred_element_type=jnp.float32,
     )
-    full_grad = lax.all_gather(bin_grad, "shell", axis=2, tiled=True)
+    full_grad = produce_orders(bin_grad)
     mixed = jnp.einsum(
         "bs,brw->srw",
         lens_weight,

time: 212 us -> 215 us (1.014)
    all_to_all x0 -> x1, blocking collectives: none -> 11.6 us  [seats_all_recover(): all_to_all(jnp.stack(row_list), 'shell', split_axis=0, concat_axis=0)]
    all_gather x1 -> x0, blocking collectives: 10.1 us -> none  [per_device(): full_grad = lax.all_gather(bin_grad, 'shell', axis=2, tiled=True)]
where the time goes in v1:
time: 215 us; the launch traced here: 213 us
  matrix products  54 us (25%)
  starting transfers between devices  42 us (20%)
  waiting for transfers between devices  40.2 us (19%)
  local copies, waits for them, and re-layouts  36.8 us (17%)
  between operations  14.2 us (7%)
  other arithmetic  13.4 us (6%)
  blocking collectives  11.6 us (5%)
    dot_general x4, matrix products, deposit_block(): jnp.einsum('gr,kgc->krc', rows_hot, spread, precision=lax.Precision.HIGHE...  26.2 us
    convert_element_type x4, local copies, waits for them, and re-layouts, deposit_block(): cols_hot = (col_of[:, None] == lax.broadcasted_iota(jnp.int32, (codes.sha...  22.3 us
    reduce_scatter x1, waiting for transfers between devices, per_device(): lax.psum_scatter(partial_bins, 'shell', scatter_dimension=2, tiled=True)  21.4 us
    dot_general x4, matrix products, deposit_block(): jnp.einsum('gr,krc->kgc', rows_hot, shear_rows, precision=lax.Precision.H...  17.6 us
    all_to_all x1, starting transfers between devices, per_device(): lax.all_to_all(lax.all_to_all(packet, 'shell', split_axis=1, concat_axis=...  13.7 us
    ppermute x4, starting transfers between devices, extended(): lax.ppermute(lax.slice_in_dim(block, 0, width, axis=dim), axis, backward)  12.5 us
    all_to_all x1, blocking collectives, seats_all_recover(): all_to_all(jnp.stack(row_list), 'shell', split_axis=0, concat_axis=0)  11.6 us
    ppermute x4, starting transfers between devices, extended(): lax.ppermute(lax.slice_in_dim(block, block.shape[dim] - width, None, axis...  11.6 us
  transfers between devices with their start and end apart: 11, of which 4 were waited for; matrix products, arithmetic and copies ran while one was open for 6% of the time, Pallas kernels for 0%

profile of v1, /device:TPU:31, one launch (start us, length us, event | category | flops | bytes accessed | tf_op | source)
XLA Modules:
  0.0 212.6 jit_solution(13942366559168624233)
XLA Ops:
  7.2 3.4 %convolution_bitcast_fusion.1 = f32[5,32,512]{2,0,1:T(8,128)} fusion(f32[16,32,512]{2,1,0:T(8,128)} %param.12, f32[16]{0:T(128)S(1)} %multiply_multiply_fusion, f32[16]{0:T(128)} %param.13, f32[5,16]{1,0:T(8,128)S(1)} %copy-done), kind=kOutput, calls=%fused_computation.44 | convolution fusion | flops 16515072 | bytes 1376704 | tf_op jit(solution)/shard_map/bs,srw->brw/dot_general | solution.py:103
  12.8 21.4 %reduce-scatter.2.cloned.1.call-done = f32[5,32,128]{2,0,1:T(8,128)} async-done(((f32[5,32,512]{2,0,1:T(8,128)}), f32[5,32,128]{2,0,1:T(8,128)}) %reduce-scatter.2.cloned.1.call-update) | async-done | bytes 81936 | tf_op jit(solution)/shard_map/reduce_scatter | solution.py:110
  36.5 3.0 %collective-permute-start.1 = (bf16[5,32,16]{2,0,1:T(8,128)(2,1)S(1)}, bf16[5,32,16]{2,0,1:T(8,128)(2,1)S(1)}, u32[]{:S(2)}, u32[]{:S(2)}) collective-permute-start(bf16[5,32,16]{2,0,1:T(8,128)(2,1)S(1)} %get-tuple-element.165), channel_id=1, source_target_pairs={{64,0},{128,64},{192,128},{65,1},{129,65},{193,129},{66,2},{130,66... | collective-permute-start | bytes 15368 | tf_op jit(solution)/shard_map/ppermute | solution.py:32
  39.6 2.1 pad_maximum_fusion
  41.7 4.2 %all-to-all-start = ((f32[4,4,64,128]{3,0,2,1:T(4,128)}), f32[4,4,64,128]{3,0,2,1:T(4,128)}, u32[]{:S(2)}, u32[]{:S(2)}) async-start(f32[4,4,64,128]{3,0,2,1:T(4,128)} %pad_maximum_fusion), calls=%async_computation | async-start | bytes 1048576 | tf_op jit(solution)/shard_map/all_to_all | solution.py:127
  46.7 4.0 %collective-permute-start.2 = (bf16[5,16,160]{2,0,1:T(8,128)(2,1)}, bf16[5,16,160]{2,0,1:T(8,128)(2,1)}, u32[]{:S(2)}, u32[]{:S(2)}) collective-permute-start(bf16[5,16,160]{2,0,1:T(8,128)(2,1)} %get-tuple-element.161), channel_id=1, source_target_pairs={{0,1},{1,2},{2,3},{3,4},{4,5},{5,6},{6,7},{7,8},{8,9},{9,10},{10,1... | collective-permute-start | bytes 76808 | tf_op jit(solution)/shard_map/ppermute | solution.py:29
  50.7 1.9 collective-permute-start.3
  53.7 1.9 copy.106
  55.6 13.7 %all-to-all-start.1 = ((f32[4,4,64,128]{3,0,1,2:T(4,128)}), f32[4,4,64,128]{3,0,1,2:T(4,128)}, u32[]{:S(2)}, u32[]{:S(2)}) async-start(f32[4,4,64,128]{3,0,1,2:T(4,128)} %copy.106), calls=%async_computation.1 | async-start | bytes 1048576 | tf_op jit(solution)/shard_map/all_to_all | solution.py:126
  71.1 1.6 fusion.34
  72.8 11.5 %all-to-all-done.1 = f32[4,4,64,128]{3,0,1,2:T(4,128)} async-done(((f32[4,4,64,128]{3,0,1,2:T(4,128)}), f32[4,4,64,128]{3,0,1,2:T(4,128)}, u32[]{:S(2)}, u32[]{:S(2)}) %all-to-all-start.1) | async-done | bytes 524320 | tf_op jit(solution)/shard_map/all_to_all | solution.py:126
  84.3 79.2 %while.16 = (s32[]{:T(128)}, f32[2,160,128]{2,1,0:T(8,128)}, f32[4,4,64,128]{3,0,1,2:T(4,128)}, f32[2,160,128]{2,1,0:T(8,128)S(1)}, s32[]{:T(128)}, /*index=5*/s32[]{:T(128)}, s32[]{}, s32[]{}) while((s32[]{:T(128)}, f32[2,160,128]{2,1,0:T(8,128)}, f32[4,4,64,128]{3,0,1,2:T(4,128)}, f32[2,160,128]{2,1,0:T(8,128)S(1)}, s32[]{:T(128)}, ...), condition=%wide.region_3.4_spmd.clone, body=%wide.region_1.3_spmd.clone.sunk | while | flops 8064376832 | bytes 40337624 | solution.py:141
  85.8 4.4 %fusion.113 = f32[8192,2]{0,1:T(2,128)S(1)} fusion(f32[8192,128]{0,1:T(8,128)S(1)} %fusion.112, f32[2,160,128]{2,1,0:T(8,128)S(1)} %get-tuple-element.218, s32[8192]{0:T(1024)S(1)} %get-tuple-element.196), kind=kOutput, calls=%fused_computation.11.clone.1 | convolution fusion | flops 4032020480 | bytes 4456448 | tf_op jit(solution)/shard_map/while/body/eval_jaxpr/gr,krc->kgc/dot_general | solution.py:64
  91.3 5.6 %copy.164 = f32[8192,128]{1,0:T(8,128)} copy(f32[8192,128]{0,1:T(8,128)} %copy-done.1) | data formatting | bytes 8388608 | tf_op jit(solution)/shard_map/while/body/eval_jaxpr/convert_element_type | solution.py:63
  96.9 6.6 %fusion.115 = f32[2,160,128]{2,1,0:T(8,128)S(1)} fusion(s32[8192]{0:T(1024)S(1)} %get-tuple-element.196, f32[8192,128]{1,0:T(8,128)} %copy.164, f32[2,8192]{1,0:T(2,128)S(1)} %fusion.114, f32[2,160,128]{2,1,0:T(8,128)S(1)} %copy-done.3, pred[]{:T(512)S(6)} %compare.19), kind=kOutput, calls=%fused_computation.13.clone.1 | convolution fusion | flops 4030021632 | bytes 4620289 | tf_op jit(solution)/shard_map/while/body/eval_jaxpr/gr,kgc->krc/dot_general | solution.py:75
  105.6 4.4 %fusion.113 = f32[8192,2]{0,1:T(2,128)S(1)} fusion(f32[8192,128]{0,1:T(8,128)S(1)} %fusion.112, f32[2,160,128]{2,1,0:T(8,128)S(1)} %get-tuple-element.218, s32[8192]{0:T(1024)S(1)} %get-tuple-element.196), kind=kOutput, calls=%fused_computation.11.clone.1 | convolution fusion | flops 4032020480 | bytes 4456448 | tf_op jit(solution)/shard_map/while/body/eval_jaxpr/gr,krc->kgc/dot_general | solution.py:64
  111.1 5.6 %copy.164 = f32[8192,128]{1,0:T(8,128)} copy(f32[8192,128]{0,1:T(8,128)} %copy-done.1) | data formatting | bytes 8388608 | tf_op jit(solution)/shard_map/while/body/eval_jaxpr/convert_element_type | solution.py:63
  116.7 6.6 %fusion.115 = f32[2,160,128]{2,1,0:T(8,128)S(1)} fusion(s32[8192]{0:T(1024)S(1)} %get-tuple-element.196, f32[8192,128]{1,0:T(8,128)} %copy.164, f32[2,8192]{1,0:T(2,128)S(1)} %fusion.114, f32[2,160,128]{2,1,0:T(8,128)S(1)} %copy-done.3, pred[]{:T(512)S(6)} %compare.19), kind=kOutput, calls=%fused_computation.13.clone.1 | convolution fusion | flops 4030021632 | bytes 4620289 | tf_op jit(solution)/shard_map/while/body/eval_jaxpr/gr,kgc->krc/dot_general | solution.py:75
  125.4 4.4 %fusion.113 = f32[8192,2]{0,1:T(2,128)S(1)} fusion(f32[8192,128]{0,1:T(8,128)S(1)} %fusion.112, f32[2,160,128]{2,1,0:T(8,128)S(1)} %get-tuple-element.218, s32[8192]{0:T(1024)S(1)} %get-tuple-element.196), kind=kOutput, calls=%fused_computation.11.clone.1 | convolution fusion | flops 4032020480 | bytes 4456448 | tf_op jit(solution)/shard_map/while/body/eval_jaxpr/gr,krc->kgc/dot_general | solution.py:64
  130.9 5.6 %copy.164 = f32[8192,128]{1,0:T(8,128)} copy(f32[8192,128]{0,1:T(8,128)} %copy-done.1) | data formatting | bytes 8388608 | tf_op jit(solution)/shard_map/while/body/eval_jaxpr/convert_element_type | solution.py:63
  136.5 6.6 %fusion.115 = f32[2,160,128]{2,1,0:T(8,128)S(1)} fusion(s32[8192]{0:T(1024)S(1)} %get-tuple-element.196, f32[8192,128]{1,0:T(8,128)} %copy.164, f32[2,8192]{1,0:T(2,128)S(1)} %fusion.114, f32[2,160,128]{2,1,0:T(8,128)S(1)} %copy-done.3, pred[]{:T(512)S(6)} %compare.19), kind=kOutput, calls=%fused_computation.13.clone.1 | convolution fusion | flops 4030021632 | bytes 4620289 | tf_op jit(solution)/shard_map/while/body/eval_jaxpr/gr,kgc->krc/dot_general | solution.py:75
  145.2 4.4 %fusion.113 = f32[8192,2]{0,1:T(2,128)S(1)} fusion(f32[8192,128]{0,1:T(8,128)S(1)} %fusion.112, f32[2,160,128]{2,1,0:T(8,128)S(1)} %get-tuple-element.218, s32[8192]{0:T(1024)S(1)} %get-tuple-element.196), kind=kOutput, calls=%fused_computation.11.clone.1 | convolution fusion | flops 4032020480 | bytes 4456448 | tf_op jit(solution)/shard_map/while/body/eval_jaxpr/gr,krc->kgc/dot_general | solution.py:64
  150.7 5.6 %copy.164 = f32[8192,128]{1,0:T(8,128)} copy(f32[8192,128]{0,1:T(8,128)} %copy-done.1) | data formatting | bytes 8388608 | tf_op jit(solution)/shard_map/while/body/eval_jaxpr/convert_element_type | solution.py:63
  156.3 6.6 %fusion.115 = f32[2,160,128]{2,1,0:T(8,128)S(1)} fusion(s32[8192]{0:T(1024)S(1)} %get-tuple-element.196, f32[8192,128]{1,0:T(8,128)} %copy.164, f32[2,8192]{1,0:T(2,128)S(1)} %fusion.114, f32[2,160,128]{2,1,0:T(8,128)S(1)} %copy-done.3, pred[]{:T(512)S(6)} %compare.19), kind=kOutput, calls=%fused_computation.13.clone.1 | convolution fusion | flops 4030021632 | bytes 4620289 | tf_op jit(solution)/shard_map/while/body/eval_jaxpr/gr,kgc->krc/dot_general | solution.py:75
  165.8 5.4 %collective-permute-start.5 = (bf16[2,5,32,16]{3,2,0,1:T(8,128)(2,1)S(1)}, bf16[2,5,32,16]{3,2,0,1:T(8,128)(2,1)S(1)}, u32[]{:S(2)}, u32[]{:S(2)}) collective-permute-start(bf16[2,5,32,16]{3,2,0,1:T(8,128)(2,1)S(1)} %get-tuple-element.163), channel_id=1, source_target_pairs={{64,0},{128,64},{192,128},{65,1},{129,65},{193,129},{66,2},{130,66... | collective-permute-start | bytes 30728 | tf_op jit(solution)/shard_map/ppermute | solution.py:32
  172.3 5.0 %collective-permute-start.6 = (bf16[2,5,16,160]{3,2,0,1:T(8,128)(2,1)S(1)}, bf16[2,5,16,160]{3,2,0,1:T(8,128)(2,1)S(1)}, u32[]{:S(2)}, u32[]{:S(2)}) collective-permute-start(bf16[2,5,16,160]{3,2,0,1:T(8,128)(2,1)S(1)} %get-tuple-element.159), channel_id=1, source_target_pairs={{0,1},{1,2},{2,3},{3,4},{4,5},{5,6},{6,7},{7,8},{8,9},{9,10},{10,1... | collective-permute-start | bytes 153608 | tf_op jit(solution)/shard_map/ppermute | solution.py:29
  177.3 2.1 %collective-permute-start.7 = (bf16[2,5,16,160]{3,2,0,1:T(8,128)(2,1)S(1)}, bf16[2,5,16,160]{3,2,0,1:T(8,128)(2,1)S(1)}, u32[]{:S(2)}, u32[]{:S(2)}) collective-permute-start(bf16[2,5,16,160]{3,2,0,1:T(8,128)(2,1)S(1)} %get-tuple-element.158), channel_id=1, source_target_pairs={{1,0},{2,1},{3,2},{4,3},{5,4},{6,5},{7,6},{8,7},{9,8},{10,9},{11,1... | collective-permute-start | bytes 153608 | tf_op jit(solution)/shard_map/ppermute | solution.py:32
  180.5 6.5 %collective-permute-done.7 = bf16[2,5,16,160]{3,2,0,1:T(8,128)(2,1)S(1)} collective-permute-done((bf16[2,5,16,160]{3,2,0,1:T(8,128)(2,1)S(1)}, bf16[2,5,16,160]{3,2,0,1:T(8,128)(2,1)S(1)}, u32[]{:S(2)}, u32[]{:S(2)}) %collective-permute-start.7) | collective-permute-done | bytes 51232 | tf_op jit(solution)/shard_map/ppermute | solution.py:32
  189.0 1.6 fusion.43
  190.6 11.6 %all_to_all.15 = f32[4,5,32,128]{3,2,1,0:T(8,128)S(1)} all-to-all(f32[4,5,32,128]{3,2,1,0:T(8,128)S(1)} %stack.279), channel_id=1, replica_groups=mesh['shell'=4,'tile'=64] {'shell'}, dimensions={0} | all-to-all | bytes 655360 | tf_op jit(solution)/shard_map/all_to_all | solution.py:17
  202.6 1.6 fusion.42
  204.2 1.6 copy.116
  (153 shorter events, 27.7 us)
Async XLA Ops:
  6.5 0.7 copy-start
  6.5 46.1 %copy-start.5 = (bf16[2,33,33]{2,0,1:T(2,128)(2,1)S(1)}, bf16[2,33,33]{2,0,1:T(2,128)(2,1)}, u32[]{:S(2)}) copy-start(bf16[2,33,33]{2,0,1:T(2,128)(2,1)} %param.15) | copy-start | bytes 13072
  6.5 27.7 %reduce-scatter.2.cloned.1.call-start = ((), (), s32[]{:S(2)}) async-start(), calls=%async_computation.4 | async-start | bytes 655360 | tf_op jit(solution)/shard_map/reduce_scatter | solution.py:110
  10.6 43.1 %copy-start.6 = (s32[32,128]{1,0:T(8,128)S(1)}, s32[32,128]{1,0:T(8,128)}, u32[]{:S(2)}) copy-start(s32[32,128]{1,0:T(8,128)} %param.16) | copy-start | bytes 49156
  35.2 10.7 %collective-permute-start = (bf16[5,32,16]{2,0,1:T(8,128)(2,1)S(1)}, bf16[5,32,16]{2,0,1:T(8,128)(2,1)S(1)}, u32[]{:S(2)}, u32[]{:S(2)}) collective-permute-start(bf16[5,32,16]{2,0,1:T(8,128)(2,1)S(1)} %get-tuple-element.164), channel_id=1, source_target_pairs={{0,64},{64,128},{128,192},{1,65},{65,129},{129,193},{2,66},{66,130... | collective-permute-start | bytes 15368 | tf_op jit(solution)/shard_map/ppermute | solution.py:29
  36.5 9.4 %collective-permute-start.1 = (bf16[5,32,16]{2,0,1:T(8,128)(2,1)S(1)}, bf16[5,32,16]{2,0,1:T(8,128)(2,1)S(1)}, u32[]{:S(2)}, u32[]{:S(2)}) collective-permute-start(bf16[5,32,16]{2,0,1:T(8,128)(2,1)S(1)} %get-tuple-element.165), channel_id=1, source_target_pairs={{64,0},{128,64},{192,128},{65,1},{129,65},{193,129},{66,2},{130,66... | collective-permute-start | bytes 15368 | tf_op jit(solution)/shard_map/ppermute | solution.py:32
  41.7 12.1 %all-to-all-start = ((f32[4,4,64,128]{3,0,2,1:T(4,128)}), f32[4,4,64,128]{3,0,2,1:T(4,128)}, u32[]{:S(2)}, u32[]{:S(2)}) async-start(f32[4,4,64,128]{3,0,2,1:T(4,128)} %pad_maximum_fusion), calls=%async_computation | async-start | bytes 1048576 | tf_op jit(solution)/shard_map/all_to_all | solution.py:127
  46.7 22.6 %collective-permute-start.2 = (bf16[5,16,160]{2,0,1:T(8,128)(2,1)}, bf16[5,16,160]{2,0,1:T(8,128)(2,1)}, u32[]{:S(2)}, u32[]{:S(2)}) collective-permute-start(bf16[5,16,160]{2,0,1:T(8,128)(2,1)} %get-tuple-element.161), channel_id=1, source_target_pairs={{0,1},{1,2},{2,3},{3,4},{4,5},{5,6},{6,7},{7,8},{8,9},{9,10},{10,1... | collective-permute-start | bytes 76808 | tf_op jit(solution)/shard_map/ppermute | solution.py:29
  50.7 18.6 %collective-permute-start.3 = (bf16[5,16,160]{2,0,1:T(8,128)(2,1)}, bf16[5,16,160]{2,0,1:T(8,128)(2,1)}, u32[]{:S(2)}, u32[]{:S(2)}) collective-permute-start(bf16[5,16,160]{2,0,1:T(8,128)(2,1)} %get-tuple-element.160), channel_id=1, source_target_pairs={{1,0},{2,1},{3,2},{4,3},{5,4},{6,5},{7,6},{8,7},{9,8},{10,9},{11,1... | collective-permute-start | bytes 76808 | tf_op jit(solution)/shard_map/ppermute | solution.py:32
  55.6 28.6 %all-to-all-start.1 = ((f32[4,4,64,128]{3,0,1,2:T(4,128)}), f32[4,4,64,128]{3,0,1,2:T(4,128)}, u32[]{:S(2)}, u32[]{:S(2)}) async-start(f32[4,4,64,128]{3,0,1,2:T(4,128)} %copy.106), calls=%async_computation.1 | async-start | bytes 1048576 | tf_op jit(solution)/shard_map/all_to_all | solution.py:126
  85.8 4.4 %copy-start.1 = (f32[8192,128]{0,1:T(8,128)}, f32[8192,128]{0,1:T(8,128)S(1)}, u32[]{:S(2)}) copy-start(f32[8192,128]{0,1:T(8,128)S(1)} %fusion.112) | copy-start | bytes 12582916 | tf_op jit(solution)/shard_map/while
  90.3 6.6 %copy-start.3 = (f32[2,160,128]{2,1,0:T(8,128)S(1)}, f32[2,160,128]{2,1,0:T(8,128)}, u32[]{:S(2)}) copy-start(f32[2,160,128]{2,1,0:T(8,128)} %get-tuple-element.208) | copy-start | bytes 491524 | tf_op jit(solution)/shard_map/while
  103.4 0.7 copy-start.4
  105.6 4.4 %copy-start.1 = (f32[8192,128]{0,1:T(8,128)}, f32[8192,128]{0,1:T(8,128)S(1)}, u32[]{:S(2)}) copy-start(f32[8192,128]{0,1:T(8,128)S(1)} %fusion.112) | copy-start | bytes 12582916 | tf_op jit(solution)/shard_map/while
  110.1 6.6 %copy-start.3 = (f32[2,160,128]{2,1,0:T(8,128)S(1)}, f32[2,160,128]{2,1,0:T(8,128)}, u32[]{:S(2)}) copy-start(f32[2,160,128]{2,1,0:T(8,128)} %get-tuple-element.208) | copy-start | bytes 491524 | tf_op jit(solution)/shard_map/while
  123.2 0.7 copy-start.4
  125.4 4.4 %copy-start.1 = (f32[8192,128]{0,1:T(8,128)}, f32[8192,128]{0,1:T(8,128)S(1)}, u32[]{:S(2)}) copy-start(f32[8192,128]{0,1:T(8,128)S(1)} %fusion.112) | copy-start | bytes 12582916 | tf_op jit(solution)/shard_map/while
  129.9 6.6 %copy-start.3 = (f32[2,160,128]{2,1,0:T(8,128)S(1)}, f32[2,160,128]{2,1,0:T(8,128)}, u32[]{:S(2)}) copy-start(f32[2,160,128]{2,1,0:T(8,128)} %get-tuple-element.208) | copy-start | bytes 491524 | tf_op jit(solution)/shard_map/while
  143.0 0.7 copy-start.4
  145.2 4.4 %copy-start.1 = (f32[8192,128]{0,1:T(8,128)}, f32[8192,128]{0,1:T(8,128)S(1)}, u32[]{:S(2)}) copy-start(f32[8192,128]{0,1:T(8,128)S(1)} %fusion.112) | copy-start | bytes 12582916 | tf_op jit(solution)/shard_map/while
  149.7 6.6 %copy-start.3 = (f32[2,160,128]{2,1,0:T(8,128)S(1)}, f32[2,160,128]{2,1,0:T(8,128)}, u32[]{:S(2)}) copy-start(f32[2,160,128]{2,1,0:T(8,128)} %get-tuple-element.208) | copy-start | bytes 491524 | tf_op jit(solution)/shard_map/while
  162.8 0.7 copy-start.4
  164.5 6.9 %collective-permute-start.4 = (bf16[2,5,32,16]{3,2,0,1:T(8,128)(2,1)S(1)}, bf16[2,5,32,16]{3,2,0,1:T(8,128)(2,1)S(1)}, u32[]{:S(2)}, u32[]{:S(2)}) collective-permute-start(bf16[2,5,32,16]{3,2,0,1:T(8,128)(2,1)S(1)} %get-tuple-element.162), channel_id=1, source_target_pairs={{0,64},{64,128},{128,192},{1,65},{65,129},{129,193},{2,66},{66,130... | collective-permute-start | bytes 30728 | tf_op jit(solution)/shard_map/ppermute | solution.py:29
  165.8 6.3 %collective-permute-start.5 = (bf16[2,5,32,16]{3,2,0,1:T(8,128)(2,1)S(1)}, bf16[2,5,32,16]{3,2,0,1:T(8,128)(2,1)S(1)}, u32[]{:S(2)}, u32[]{:S(2)}) collective-permute-start(bf16[2,5,32,16]{3,2,0,1:T(8,128)(2,1)S(1)} %get-tuple-element.163), channel_id=1, source_target_pairs={{64,0},{128,64},{192,128},{65,1},{129,65},{193,129},{66,2},{130,66... | collective-permute-start | bytes 30728 | tf_op jit(solution)/shard_map/ppermute | solution.py:32
  172.3 8.2 %collective-permute-start.6 = (bf16[2,5,16,160]{3,2,0,1:T(8,128)(2,1)S(1)}, bf16[2,5,16,160]{3,2,0,1:T(8,128)(2,1)S(1)}, u32[]{:S(2)}, u32[]{:S(2)}) collective-permute-start(bf16[2,5,16,160]{3,2,0,1:T(8,128)(2,1)S(1)} %get-tuple-element.159), channel_id=1, source_target_pairs={{0,1},{1,2},{2,3},{3,4},{4,5},{5,6},{6,7},{7,8},{8,9},{9,10},{10,1... | collective-permute-start | bytes 153608 | tf_op jit(solution)/shard_map/ppermute | solution.py:29
  177.3 9.7 %collective-permute-start.7 = (bf16[2,5,16,160]{3,2,0,1:T(8,128)(2,1)S(1)}, bf16[2,5,16,160]{3,2,0,1:T(8,128)(2,1)S(1)}, u32[]{:S(2)}, u32[]{:S(2)}) collective-permute-start(bf16[2,5,16,160]{3,2,0,1:T(8,128)(2,1)S(1)} %get-tuple-element.158), channel_id=1, source_target_pairs={{1,0},{2,1},{3,2},{4,3},{5,4},{6,5},{7,6},{8,7},{9,8},{10,9},{11,1... | collective-permute-start | bytes 153608 | tf_op jit(solution)/shard_map/ppermute | solution.py:32
  189.0 13.6 %copy-start.2 = (f32[16,32,512]{2,1,0:T(8,128)S(1)}, f32[16,32,512]{2,1,0:T(8,128)}, u32[]{:S(2)}) copy-start(f32[16,32,512]{2,1,0:T(8,128)} %param.12) | copy-start | bytes 3145732
  189.0 13.6 %copy-start.7 = (f32[16]{0:T(128)S(1)}, f32[16]{0:T(128)}, u32[]{:S(2)}) copy-start(f32[16]{0:T(128)} %param.13) | copy-start | bytes 196
Sparse Core Ops, SparseCore 0:
  10.7 23.4 reduce-scatter.1
